TPU v7x, 256 devices: a whole 4x4x8 slice. The times are simulated.
256 devices in a mesh: dp: 2 (over core), ctx: 8 (over y, z_lo), feat: 16 (over x, z_hi).
Axes of the slice: x: 4, y: 4, z: 8 (z_hi: 4, z_lo: 2; z = z_hi * 2 + z_lo), core: 2. Of those that a mesh axis runs over, the one named last changes fastest.
Arguments:
- out_grads: bfloat16 [2048, 28672], P(('dp', 'ctx'), 'feat'), may hold values from -6 to 6
- acts: bfloat16 [2048, 8192], P(('dp', 'ctx'), 'feat'), may hold values from -6 to 6
- domain_ids: int32 [2048], P(('dp', 'ctx')), may hold values from 0 to 7
- domain_weights: int32 [8], replicated, may hold values from 1 to 4
Outputs:
- grad_factor: bfloat16 [28672, 28672], P(('dp', 'ctx'), 'feat')
- act_factor: bfloat16 [8192, 8192], P(('dp', 'ctx'), 'feat')
All inputs are finite; a program needn't handle non-finite values.
Results may differ from a plain program's by a relative error of at most 0.003.
Values may be sent and summed in bfloat16 or wider, within the bound.
No kernel may reach another device: no remote copies, remote signals or barrier semaphores. Data moves between devices by JAX's collectives and lax.ppermute only.
A program may use at most 128 MiB of HBM per device.

v0:
```python
import jax
import jax.numpy as jnp
from jax import lax
from jax.sharding import PartitionSpec as P


def from_root(block, axis, owner):
    block = jnp.where(lax.axis_index(axis) == owner, block, jnp.zeros_like(block))
    return lax.psum(block, axis)


def weigh_rows(tok_ids, rows, domain_weights):
    labels = jnp.arange(domain_weights.shape[0], dtype=jnp.int32)
    match = tok_ids[:, None] == labels[None, :]
    tok_weight = jnp.sum(jnp.where(match, domain_weights[None, :], 0), axis=1).astype(jnp.float32)
    return (tok_weight[:, None] * rows.astype(jnp.float32)).astype(jnp.bfloat16)


def contract_tokens(left, right):
    return lax.dot_general(
        left, right, (((0,), (0,)), ((), ())), preferred_element_type=jnp.float32
    )


def local(out_grads, acts, domain_ids, domain_weights):
    group_size = lax.axis_size(("dp", "ctx"))
    inv_count = 1.0 / (out_grads.shape[0] * group_size)
    all_grads, all_acts, all_ids = (
        lax.all_gather(out_grads, ("dp", "ctx"), axis=0, tiled=True),
        lax.all_gather(acts, ("dp", "ctx"), axis=0, tiled=True),
        lax.all_gather(domain_ids, ("dp", "ctx"), axis=0, tiled=True),
    )
    tile_ratio = lax.axis_size("feat") // group_size
    first_root = lax.axis_index(("dp", "ctx")) * tile_ratio
    copy_grads = from_root(all_grads, "feat", first_root + 0)
    copy_acts = from_root(all_acts, "feat", first_root + 0)
    grad_sum = contract_tokens(copy_grads, weigh_rows(all_ids, all_grads, domain_weights))
    act_sum = contract_tokens(copy_acts, weigh_rows(all_ids, all_acts, domain_weights))
    grad_factor = (grad_sum * inv_count).astype(jnp.bfloat16)
    act_factor = (act_sum * inv_count).astype(jnp.bfloat16)
    return (grad_factor, act_factor)


def solution(mesh):
    in_specs = (P(("dp", "ctx"), "feat"), P(("dp", "ctx"), "feat"), P(("dp", "ctx")), P())
    out_specs = (P(("dp", "ctx"), "feat"), P(("dp", "ctx"), "feat"))
    return jax.shard_map(local, mesh=mesh, in_specs=in_specs, out_specs=out_specs, check_vma=False)
```

profile of v0, /device:TPU:41, one launch (start us, length us, event | category | flops | bytes accessed | tf_op | source)
XLA Modules:
  0.0 559.2 jit_solution(695061584460823528)
XLA Ops:
  7.2 0.0 all-gather.6.cloned.1.call-start
  7.2 0.7 all-gather.6.cloned.1.call-update
  7.9 0.0 all-gather.4.cloned.1.call-start
  7.9 0.7 all-gather.4.cloned.1.call-update
  8.6 0.0 all-reduce.3.cloned.1.call-start
  8.7 39.6 %all-gather.6.cloned.1.call-done = bf16[2048,512]{1,0:T(8,128)(2,1)} async-done(((bf16[128,512]{1,0:T(8,128)(2,1)}), bf16[2048,512]{1,0:T(8,128)(2,1)}) %all-gather.6.cloned.1.call-update) | async-done | bytes 2097168 | tf_op jit(solution)/shard_map/all_gather | solution.py:30
  48.3 1.5 broadcast_select_fusion.1
  49.8 51.1 %all-gather.4.cloned.1.call-done = bf16[2048,1792]{1,0:T(8,128)(2,1)} async-done(((bf16[128,1792]{1,0:T(8,128)(2,1)}), bf16[2048,1792]{1,0:T(8,128)(2,1)}) %all-gather.4.cloned.1.call-update) | async-done | bytes 7340048 | tf_op jit(solution)/shard_map/all_gather | solution.py:29
  100.9 3.4 broadcast_select_fusion
  104.3 0.0 copy-start.1
  104.3 0.0 copy-start.2
  104.3 0.0 all-reduce.3.cloned.1.call-update
  104.3 0.6 copy-done.1
  104.9 25.4 %all-gather = s32[16,1,128]{2,1,0:T(1,128)S(1)} all-gather(s32[1,1,128]{2,1,0:T(1,128)S(1)} %bitcast.5), channel_id=1, replica_groups=mesh['dp'=2,'ctx'=8,'feat'=16] {'dp','ctx'}, dimensions={0}, use_global_device_ids=true | all-gather | bytes 8704 | tf_op jit(solution)/shard_map/all_gather | solution.py:31
  130.3 0.0 copy-done.2
  130.3 0.1 select_reduce_fusion
  130.4 399.4 %all-reduce.3.cloned.1.call-done = (bf16[2048,1792]{1,0:T(8,128)(2,1)}, bf16[2048,512]{1,0:T(8,128)(2,1)}) async-done(((bf16[2048,1792]{1,0:T(8,128)(2,1)}, bf16[2048,512]{1,0:T(8,128)(2,1)}), (bf16[2048,1792]{1,0:T(8,128)(2,1)}, bf16[2048,512]{1,0:T(8,128)(2,1)})) %all-reduce.3.cloned.1.call-update) | async-done | bytes 9437200 | tf_op jit(solution)/shard_map/psum | solution.py:9
  529.8 0.0 copy-start
  529.8 0.0 copy-start.3
  529.8 20.7 %multiply_convert_fusion.1 = bf16[1792,1792]{1,0:T(8,128)(2,1)} fusion(bf16[2048,1792]{1,0:T(8,128)(2,1)} %get-tuple-element.2, bf16[2048,1792]{1,0:T(8,128)(2,1)} %all-gather.4.cloned.1.call-done, f32[2048]{0:T(1024)S(1)} %convert_element_type.26), kind=kOutput, calls=%fused_computation.1 | convolution fusion | flops 13170769920 | bytes 21110784 | tf_op jit(solution)/shard_map/dot_general | solution.py:20
  550.5 0.0 copy-done
  550.5 0.0 copy-done.3
  550.5 2.1 fusion.4
  (1 shorter events, 0.0 us)
Async XLA Ops:
  7.2 41.2 %all-gather.6.cloned.1.call-start = ((), (), s32[]{:S(2)}) async-start(), calls=%async_computation.1 | async-start | bytes 2228224 | tf_op jit(solution)/shard_map/all_gather | solution.py:30
  7.9 93.0 %all-gather.4.cloned.1.call-start = ((), (), s32[]{:S(2)}) async-start(), calls=%async_computation | async-start | bytes 7798784 | tf_op jit(solution)/shard_map/all_gather | solution.py:29
  8.6 521.1 %all-reduce.3.cloned.1.call-start = ((), (), s32[]{:S(2)}) async-start(), calls=%async_computation.2 | async-start | bytes 18874368 | tf_op jit(solution)/shard_map/psum | solution.py:9
  104.3 0.7 copy-start.1
  104.3 26.0 %copy-start.2 = (s32[8]{0:T(128)S(1)}, s32[8]{0:T(128)}, u32[]{:S(2)}) copy-start(s32[8]{0:T(128)} %param.7) | copy-start | bytes 100
  529.8 20.7 %copy-start = (bf16[2048,512]{1,0:T(8,128)(2,1)S(1)}, bf16[2048,512]{1,0:T(8,128)(2,1)}, u32[]{:S(2)}) copy-start(bf16[2048,512]{1,0:T(8,128)(2,1)} %all-gather.6.cloned.1.call-done) | copy-start | bytes 6291460
  529.8 20.7 %copy-start.3 = (bf16[2048,512]{1,0:T(8,128)(2,1)S(1)}, bf16[2048,512]{1,0:T(8,128)(2,1)}, u32[]{:S(2)}) copy-start(bf16[2048,512]{1,0:T(8,128)(2,1)} %get-tuple-element.3) | copy-start | bytes 6291460
Sparse Core Ops, SparseCore 0:
  9.9 38.4 all-gather.5
  50.2 50.6 all-gather.3
  104.4 425.3 all-reduce.2
where the time goes:
time: 559 us
  waiting for transfers between devices  491 us (88%)
  blocking collectives  25.4 us (5%)
  matrix products  22.9 us (4%)
  between operations  13.8 us (2%)
    psum x1, waiting for transfers between devices, from_root(): return lax.psum(block, axis)  399 us
    all_gather x1, waiting for transfers between devices, local(): lax.all_gather(out_grads, ('dp', 'ctx'), axis=0, tiled=True)  51.1 us
    all_gather x1, waiting for transfers between devices, local(): lax.all_gather(acts, ('dp', 'ctx'), axis=0, tiled=True)  39.6 us
    all_gather x1, blocking collectives, local(): lax.all_gather(domain_ids, ('dp', 'ctx'), axis=0, tiled=True)  25.4 us
    dot_general x2, matrix products, contract_tokens(): lax.dot_general(left, right, (((0,), (0,)), ((), ())), preferred_element_...  22.9 us
  transfers between devices with their start and end apart: 3, of which 3 were waited for; matrix products, arithmetic and copies ran while one was open for 0% of the time, Pallas kernels for 0%

commit v1 on v0

--- a/solution.py
+++ b/solution.py
@@ -27,7 +27,10 @@
     inv_count = 1.0 / (out_grads.shape[0] * group_size)
     all_grads, all_acts, all_ids = (
         lax.all_gather(out_grads, ("dp", "ctx"), axis=0, tiled=True),
-        lax.all_gather(acts, ("dp", "ctx"), axis=0, tiled=True),
+        jnp.concatenate(
+            lax.all_to_all(jnp.stack([acts] * lax.axis_size(("dp", "ctx"))), ("dp", "ctx"), 0, 0),
+            axis=0,
+        ),
         lax.all_gather(domain_ids, ("dp", "ctx"), axis=0, tiled=True),
     )
     tile_ratio = lax.axis_size("feat") // group_size

time: 559 us -> 540 us (0.966)
  waiting for transfers between devices: 491 us -> 462 us
  starting transfers between devices: 0.11 us -> 6.22 us
    all_gather x1 -> x0, waiting for transfers between devices: 39.6 us -> none  [local(): lax.all_gather(acts, ('dp', 'ctx'), axis=0, tiled=True)]
    all_to_all x0 -> x1, waiting for transfers between devices: none -> 34 us  [local(): lax.all_to_all(jnp.stack([acts] * lax.axis_size(('dp', 'ctx'))), ('dp', '...]
    all_gather x1, waiting for transfers between devices: 51.1 us -> 25.8 us  [local(): lax.all_gather(out_grads, ('dp', 'ctx'), axis=0, tiled=True)]
    all_to_all x0 -> x1, starting transfers between devices: none -> 6.15 us  [local(): lax.all_to_all(jnp.stack([acts] * lax.axis_size(('dp', 'ctx'))), ('dp', '...]
  transfers between devices with their start and end apart: 3 -> 3, of which waited for: 3 -> 3; matrix products, arithmetic and copies ran while one was open for 0% -> 1% of each run, Pallas kernels for 0% -> 0%
where the time goes in v1:
time: 540 us
  waiting for transfers between devices  462 us (86%)
  blocking collectives  25.3 us (5%)
  matrix products  24.3 us (4%)
  between operations  14.1 us (3%)
  starting transfers between devices  6.22 us (1%)
    psum x1, waiting for transfers between devices, from_root(): return lax.psum(block, axis)  402 us
    all_to_all x1, waiting for transfers between devices, local(): lax.all_to_all(jnp.stack([acts] * lax.axis_size(('dp', 'ctx'))), ('dp', '...  34 us
    all_gather x1, waiting for transfers between devices, local(): lax.all_gather(out_grads, ('dp', 'ctx'), axis=0, tiled=True)  25.8 us
    all_gather x1, blocking collectives, local(): lax.all_gather(domain_ids, ('dp', 'ctx'), axis=0, tiled=True)  25.3 us
    dot_general x2, matrix products, contract_tokens(): lax.dot_general(left, right, (((0,), (0,)), ((), ())), preferred_element_...  24.3 us
  transfers between devices with their start and end apart: 3, of which 3 were waited for; matrix products, arithmetic and copies ran while one was open for 1% of the time, Pallas kernels for 0%

profile of v1, /device:TPU:41, one launch (start us, length us, event | category | flops | bytes accessed | tf_op | source)
XLA Modules:
  0.0 540.2 jit_solution(52417833540150488)
XLA Ops:
  7.2 0.0 all-gather.3.cloned.1.call-start
  7.2 0.7 all-gather.3.cloned.1.call-update
  7.9 2.4 stack.2
  10.3 6.1 %all-to-all-start = ((bf16[16,128,512]{2,1,0:T(8,128)(2,1)}), bf16[16,128,512]{2,1,0:T(8,128)(2,1)S(1)}, u32[]{:S(2)}, u32[]{:S(2)}) async-start(bf16[16,128,512]{2,1,0:T(8,128)(2,1)} %stack.2), calls=%async_computation | async-start | bytes 4194304 | tf_op jit(solution)/shard_map/all_to_all | solution.py:31
  16.5 0.0 all-reduce.3.cloned.1.call-start
  16.5 34.0 %all-to-all-done = bf16[16,128,512]{2,1,0:T(8,128)(2,1)S(1)} async-done(((bf16[16,128,512]{2,1,0:T(8,128)(2,1)}), bf16[16,128,512]{2,1,0:T(8,128)(2,1)S(1)}, u32[]{:S(2)}, u32[]{:S(2)}) %all-to-all-start) | async-done | bytes 2097184 | tf_op jit(solution)/shard_map/all_to_all | solution.py:31
  50.5 1.5 broadcast_select_fusion.1
  52.0 25.8 %all-gather.3.cloned.1.call-done = bf16[2048,1792]{1,0:T(8,128)(2,1)} async-done(((bf16[128,1792]{1,0:T(8,128)(2,1)}), bf16[2048,1792]{1,0:T(8,128)(2,1)}) %all-gather.3.cloned.1.call-update) | async-done | bytes 7340048 | tf_op jit(solution)/shard_map/all_gather | solution.py:29
  77.8 3.4 broadcast_select_fusion
  81.2 0.0 copy-start
  81.2 0.0 copy-start.1
  81.2 0.0 all-reduce.3.cloned.1.call-update
  81.3 0.6 copy-done
  81.9 25.3 %all-gather = s32[16,1,128]{2,1,0:T(1,128)S(1)} all-gather(s32[1,1,128]{2,1,0:T(1,128)S(1)} %bitcast.10), channel_id=1, replica_groups=mesh['dp'=2,'ctx'=8,'feat'=16] {'dp','ctx'}, dimensions={0}, use_global_device_ids=true | all-gather | bytes 8704 | tf_op jit(solution)/shard_map/all_gather | solution.py:34
  107.2 0.0 copy-done.1
  107.2 0.1 select_reduce_fusion
  107.3 401.7 %all-reduce.3.cloned.1.call-done = (bf16[2048,1792]{1,0:T(8,128)(2,1)}, bf16[2048,512]{1,0:T(8,128)(2,1)}) async-done(((bf16[2048,1792]{1,0:T(8,128)(2,1)}, bf16[2048,512]{1,0:T(8,128)(2,1)}), (bf16[2048,1792]{1,0:T(8,128)(2,1)}, bf16[2048,512]{1,0:T(8,128)(2,1)})) %all-reduce.3.cloned.1.call-update) | async-done | bytes 9437200 | tf_op jit(solution)/shard_map/psum | solution.py:9
  509.1 3.7 fusion.8
  512.8 20.6 %multiply_convert_fusion.1 = bf16[1792,1792]{1,0:T(8,128)(2,1)} fusion(bf16[2048,1792]{1,0:T(8,128)(2,1)} %get-tuple-element.2, bf16[2048,1792]{1,0:T(8,128)(2,1)} %all-gather.3.cloned.1.call-done, f32[2048]{0:T(1024)S(1)} %convert_element_type.29), kind=kOutput, calls=%fused_computation.1 | convolution fusion | flops 13170769920 | bytes 21110784 | tf_op jit(solution)/shard_map/dot_general | solution.py:20
  (1 shorter events, 0.0 us)
Async XLA Ops:
  7.2 70.6 %all-gather.3.cloned.1.call-start = ((), (), s32[]{:S(2)}) async-start(), calls=%async_computation.1 | async-start | bytes 7798784 | tf_op jit(solution)/shard_map/all_gather | solution.py:29
  10.3 40.2 %all-to-all-start = ((bf16[16,128,512]{2,1,0:T(8,128)(2,1)}), bf16[16,128,512]{2,1,0:T(8,128)(2,1)S(1)}, u32[]{:S(2)}, u32[]{:S(2)}) async-start(bf16[16,128,512]{2,1,0:T(8,128)(2,1)} %stack.2), calls=%async_computation | async-start | bytes 4194304 | tf_op jit(solution)/shard_map/all_to_all | solution.py:31
  16.5 492.6 %all-reduce.3.cloned.1.call-start = ((), (), s32[]{:S(2)}) async-start(), calls=%async_computation.2 | async-start | bytes 18874368 | tf_op jit(solution)/shard_map/psum | solution.py:9
  81.2 0.7 copy-start
  81.2 26.0 %copy-start.1 = (s32[8]{0:T(128)S(1)}, s32[8]{0:T(128)}, u32[]{:S(2)}) copy-start(s32[8]{0:T(128)} %param.7) | copy-start | bytes 100
Sparse Core Ops, SparseCore 0:
  9.8 67.9 all-gather.2
  81.4 427.6 all-reduce.2
